TPU v7x, 512 devices: a whole 4x8x8 slice. The times are simulated.
512 devices in a mesh: frame: 8 (over y), space: 32 (over z, x), dp: 2 (over core).
Axes of the slice: x: 4, y: 8, z: 8, core: 2. Of those that a mesh axis runs over, the one named last changes fastest.
Arguments:
- frames_in: bfloat16 [16, 4096, 768], P(('dp', 'frame'), 'space'), parts along dimension 0, may hold values from -6 to 6
- cotangent: bfloat16 [16, 4096, 768], P(('dp', 'frame'), 'space'), parts along dimension 0, may hold values from -6 to 6
- w_qkv_space: bfloat16 [768, 2304], P('space'), may hold values from -0.21875 to 0.21875
- w_out_space: bfloat16 [768, 768], P('space'), may hold values from -0.875 to 0.875
- w_qkv_time: bfloat16 [768, 2304], P('space'), may hold values from -0.21875 to 0.21875
- w_out_time: bfloat16 [768, 768], P('space'), may hold values from -0.21875 to 0.21875
- neighbours: int32 [32, 4], replicated, may hold values from 0 to 31, as said below
Outputs:
- frames_out: bfloat16 [16, 4096, 768], P(('dp', 'frame'), 'space'), parts along dimension 0
- grad_frames: bfloat16 [16, 4096, 768], P(('dp', 'frame'), 'space'), parts along dimension 0
There are 2 independent parts, one for each index of `dp`. A program takes and returns all parts, laid end to end along the dimension named above; an argument that names none is the same for every part. Nothing has to cross between parts.
Inputs may be any that keep to these rules, and one draw needn't show every extreme that they name: `neighbours`: row b lists block b first; every entry c satisfies |c - b| <= 1; entries may repeat, and a repeated entry counts once.
All inputs are finite; a program needn't handle non-finite values.
Results may differ from a plain program's by a relative error of at most 0.023.
Values may be sent and summed in bfloat16 or wider, within the bound.
No kernel may reach another device: no remote copies, remote signals or barrier semaphores. Data moves between devices by JAX's collectives and lax.ppermute only.
A program may use at most 64 MiB of HBM per device.

v0:
```python
import jax
import jax.numpy as jnp
from jax import lax
from jax.sharding import PartitionSpec as P

HEADS = 12
HD = 64
BLOCK = 128
EPS = 1e-06


def padded(cells, sides, width):
    for axis, dim in sides:
        count = lax.axis_size(axis)
        ends = count - 1
        head = lax.slice_in_dim(cells, 0, width, axis=dim)
        tail = lax.slice_in_dim(cells, cells.shape[dim] - width, cells.shape[dim], axis=dim)
        cells = jnp.concatenate(
            [
                lax.ppermute(tail, axis, [(i, (i + 1) % count) for i in range(ends)]),
                cells,
                lax.ppermute(head, axis, [((i + 1) % count, i) for i in range(ends)]),
            ],
            axis=dim,
        )
    return cells


def rms_norm(row_data):
    values = row_data.astype(jnp.float32)
    factor = lax.rsqrt(jnp.mean(values * values, axis=-1, keepdims=True) + EPS)
    return (values * factor).astype(jnp.bfloat16)


def rms_back(row_data, upstream):
    values = row_data.astype(jnp.float32)
    factor = lax.rsqrt(jnp.mean(values * values, axis=-1, keepdims=True) + EPS)
    inner_mean = jnp.mean(values * upstream, axis=-1, keepdims=True)
    return factor * upstream - values * factor**3 * inner_mean


def block_mask(neighbour_rows, first_id):
    block_count = neighbour_rows.shape[0]
    candidate = first_id + jnp.arange(3 * block_count, dtype=jnp.int32)
    matches = jnp.any(neighbour_rows[:, :, None] == candidate[None, None, :], axis=1)
    return jnp.repeat(jnp.repeat(matches, BLOCK, axis=0), BLOCK, axis=1)


def space_attend(queries, key_rows, value_rows, allowed):
    score_scale = HD ** (-0.5)
    query_count = queries.shape[0]
    key_count = key_rows.shape[0]
    output_list = []
    total_list = []
    for head_pair in range(HEADS // 2):
        start_col = head_pair * 2 * HD
        stop_col = start_col + 2 * HD
        query_part = queries[:, start_col:stop_col].reshape(query_count, 2, HD)
        key_part = key_rows[:, start_col:stop_col].reshape(key_count, 2, HD)
        value_part = value_rows[:, start_col:stop_col].reshape(key_count, 2, HD)
        scores = (
            jnp.einsum("sgh,tgh->gst", query_part, key_part, preferred_element_type=jnp.float32)
            * score_scale
        )
        exponent = jnp.where(allowed[None], jnp.exp(scores), 0.0)
        totals = jnp.sum(exponent, axis=-1)
        probability = (exponent / totals[:, :, None]).astype(jnp.bfloat16)
        combined = jnp.einsum(
            "gst,tgh->sgh", probability, value_part, preferred_element_type=jnp.float32
        )
        output_list.append(combined.astype(jnp.bfloat16).reshape(query_count, 2 * HD))
        total_list.append(totals)
    return (jnp.concatenate(output_list, axis=1), jnp.concatenate(total_list, axis=0))


def space_back(queries, key_rows, value_rows, allowed, totals, attended, grad_attended):
    score_scale = HD ** (-0.5)
    query_count = queries.shape[0]
    key_count = key_rows.shape[0]
    query_list = []
    key_list = []
    value_list = []
    for head_pair in range(HEADS // 2):
        start_col = head_pair * 2 * HD
        stop_col = start_col + 2 * HD
        query_part = queries[:, start_col:stop_col].reshape(query_count, 2, HD)
        key_part = key_rows[:, start_col:stop_col].reshape(key_count, 2, HD)
        value_part = value_rows[:, start_col:stop_col].reshape(key_count, 2, HD)
        out_part = attended[:, start_col:stop_col].reshape(query_count, 2, HD)
        grad_part = grad_attended[:, start_col:stop_col].reshape(query_count, 2, HD)
        scores = (
            jnp.einsum("sgh,tgh->gst", query_part, key_part, preferred_element_type=jnp.float32)
            * score_scale
        )
        exponent = jnp.where(allowed[None], jnp.exp(scores), 0.0)
        weight = exponent / totals[2 * head_pair : 2 * head_pair + 2, :, None]
        probability = weight.astype(jnp.bfloat16)
        prob_grad = jnp.einsum(
            "sgh,tgh->gst", grad_part, value_part, preferred_element_type=jnp.float32
        )
        row_delta = jnp.einsum(
            "sgh,sgh->gs", grad_part, out_part, preferred_element_type=jnp.float32
        )
        score_grad = (weight * (prob_grad - row_delta[:, :, None])).astype(jnp.bfloat16)
        query_grad = (
            jnp.einsum("gst,tgh->sgh", score_grad, key_part, preferred_element_type=jnp.float32)
            * score_scale
        )
        key_grad = (
            jnp.einsum("gst,sgh->tgh", score_grad, query_part, preferred_element_type=jnp.float32)
            * score_scale
        )
        value_grad = jnp.einsum(
            "gst,sgh->tgh", probability, grad_part, preferred_element_type=jnp.float32
        )
        query_list.append(query_grad.astype(jnp.bfloat16).reshape(query_count, 2 * HD))
        key_list.append(key_grad.reshape(key_count, 2 * HD))
        value_list.append(value_grad.reshape(key_count, 2 * HD))
    return (
        jnp.concatenate(query_list, axis=1),
        jnp.concatenate(key_list, axis=1),
        jnp.concatenate(value_list, axis=1),
    )


def time_attend(queries, key_rows, value_rows):
    frame_count, position_count, feature_count = queries.shape
    split_shape = (frame_count, position_count, HEADS, HD)
    score_scale = HD ** (-0.5)
    scores = (
        jnp.einsum(
            "fphd,gphd->phfg",
            queries.reshape(split_shape),
            key_rows.reshape(split_shape),
            preferred_element_type=jnp.float32,
        )
        * score_scale
    )
    causal = jnp.arange(frame_count)[:, None] >= jnp.arange(frame_count)[None, :]
    exponent = jnp.where(causal, jnp.exp(scores), 0.0)
    totals = jnp.sum(exponent, axis=-1)
    probability = (exponent / totals[..., None]).astype(jnp.bfloat16)
    combined = jnp.einsum(
        "phfg,gphd->fphd",
        probability,
        value_rows.reshape(split_shape),
        preferred_element_type=jnp.float32,
    )
    return (
        combined.astype(jnp.bfloat16).reshape(frame_count, position_count, feature_count),
        totals,
    )


def time_back(queries, key_rows, value_rows, attended, grad_attended, totals):
    frame_count, position_count, feature_count = queries.shape
    split_shape = (frame_count, position_count, HEADS, HD)
    score_scale = HD ** (-0.5)
    query_four = queries.reshape(split_shape)
    key_four = key_rows.reshape(split_shape)
    value_four = value_rows.reshape(split_shape)
    out_four = attended.reshape(split_shape)
    grad_four = grad_attended.reshape(split_shape)
    scores = (
        jnp.einsum("fphd,gphd->phfg", query_four, key_four, preferred_element_type=jnp.float32)
        * score_scale
    )
    causal = jnp.arange(frame_count)[:, None] >= jnp.arange(frame_count)[None, :]
    exponent = jnp.where(causal, jnp.exp(scores), 0.0)
    weight = exponent / totals[..., None]
    probability = weight.astype(jnp.bfloat16)
    prob_grad = jnp.einsum(
        "fphd,gphd->phfg", grad_four, value_four, preferred_element_type=jnp.float32
    )
    row_delta = jnp.einsum(
        "fphd,fphd->phf", grad_four, out_four, preferred_element_type=jnp.float32
    )
    score_grad = (weight * (prob_grad - row_delta[..., None])).astype(jnp.bfloat16)
    query_grad = (
        jnp.einsum("phfg,gphd->fphd", score_grad, key_four, preferred_element_type=jnp.float32)
        * score_scale
    )
    key_grad = (
        jnp.einsum("phfg,fphd->gphd", score_grad, query_four, preferred_element_type=jnp.float32)
        * score_scale
    )
    value_grad = jnp.einsum(
        "phfg,fphd->gphd", probability, grad_four, preferred_element_type=jnp.float32
    )
    pieces = [
        gradient.astype(jnp.bfloat16).reshape(frame_count, position_count, feature_count)
        for gradient in (query_grad, key_grad, value_grad)
    ]
    return jnp.concatenate(pieces, axis=-1)


def to_frames(local_rows):
    return lax.all_to_all(local_rows[None], "frame", split_axis=1, concat_axis=0, tiled=True)


def to_space(frame_rows):
    return lax.all_to_all(frame_rows, "frame", split_axis=0, concat_axis=1, tiled=True)[0]


def rim(first_part, second_part, width):
    return (padded(first_part, (("space", 0),), width), padded(second_part, (("space", 0),), width))


def local(frames_in, cotangent, w_qkv_space, w_out_space, w_qkv_time, w_out_time, neighbours):
    local_in = frames_in[0]
    grad_out = cotangent[0]
    shard, feature_count = local_in.shape
    weight_rows = jnp.concatenate([w_qkv_space, w_out_space, w_qkv_time, w_out_time], axis=1)
    all_weights = lax.all_gather(weight_rows, "space", axis=0, tiled=True)
    widths = [w_qkv_space.shape[1], w_out_space.shape[1], w_qkv_time.shape[1], w_out_time.shape[1]]
    bounds = [0]
    for width in widths:
        bounds.append(bounds[-1] + width)
    full_qkv_space, full_out_space, full_qkv_time, full_out_time = (
        all_weights[:, bounds[index] : bounds[index + 1]] for index in range(4)
    )
    block_count = shard // BLOCK
    space_index = lax.axis_index("space")
    lists_here = lax.dynamic_slice_in_dim(neighbours, space_index * block_count, block_count, 0)
    allowed = block_mask(lists_here, (space_index - 1) * block_count)
    normed_space = rms_norm(local_in)
    projected = jnp.dot(normed_space, full_qkv_space, preferred_element_type=jnp.float32).astype(
        jnp.bfloat16
    )
    queries = projected[:, :feature_count]
    key_window, value_window = rim(
        projected[:, feature_count : 2 * feature_count], projected[:, 2 * feature_count :], shard
    )
    attended, totals = space_attend(queries, key_window, value_window, allowed)
    update = jnp.dot(attended, full_out_space, preferred_element_type=jnp.float32)
    stream = (local_in.astype(jnp.float32) + update).astype(jnp.bfloat16)
    normed_time = rms_norm(stream)
    projected_time = jnp.dot(normed_time, full_qkv_time, preferred_element_type=jnp.float32).astype(
        jnp.bfloat16
    )
    time_rows = to_frames(projected_time)
    query_time = time_rows[..., :feature_count]
    key_time = time_rows[..., feature_count : 2 * feature_count]
    value_time = time_rows[..., 2 * feature_count :]
    attended_time, totals_time = time_attend(query_time, key_time, value_time)
    attended_back = to_space(attended_time)
    update_time = jnp.dot(attended_back, full_out_time, preferred_element_type=jnp.float32)
    frames_out = (stream.astype(jnp.float32) + update_time).astype(jnp.bfloat16)
    grad_att_time = jnp.dot(grad_out, full_out_time.T, preferred_element_type=jnp.float32).astype(
        jnp.bfloat16
    )
    grad_time_rows = to_frames(grad_att_time)
    gradients = time_back(
        query_time, key_time, value_time, attended_time, grad_time_rows, totals_time
    )
    grad_project_time = to_space(gradients)
    grad_normed_time = jnp.dot(
        grad_project_time, full_qkv_time.T, preferred_element_type=jnp.float32
    )
    grad_stream = (grad_out.astype(jnp.float32) + rms_back(stream, grad_normed_time)).astype(
        jnp.bfloat16
    )
    grad_attended = jnp.dot(
        grad_stream, full_out_space.T, preferred_element_type=jnp.float32
    ).astype(jnp.bfloat16)
    grad_query, key_partial, value_partial = space_back(
        queries, key_window, value_window, allowed, totals, attended, grad_attended
    )
    key_send = jnp.concatenate([key_partial[:shard], key_partial[2 * shard :]], axis=0).astype(
        jnp.bfloat16
    )
    value_send = jnp.concatenate(
        [value_partial[:shard], value_partial[2 * shard :]], axis=0
    ).astype(jnp.bfloat16)
    key_got, value_got = rim(key_send, value_send, shard)
    grad_key = (
        key_partial[shard : 2 * shard]
        + key_got[:shard].astype(jnp.float32)
        + key_got[3 * shard :].astype(jnp.float32)
    ).astype(jnp.bfloat16)
    grad_value = (
        value_partial[shard : 2 * shard]
        + value_got[:shard].astype(jnp.float32)
        + value_got[3 * shard :].astype(jnp.float32)
    ).astype(jnp.bfloat16)
    grad_project = jnp.concatenate([grad_query, grad_key, grad_value], axis=1)
    grad_normed = jnp.dot(grad_project, full_qkv_space.T, preferred_element_type=jnp.float32)
    grad_in = (grad_stream.astype(jnp.float32) + rms_back(local_in, grad_normed)).astype(
        jnp.bfloat16
    )
    return (frames_out[None], grad_in[None])


def solution(mesh):
    in_specs = (
        P(("dp", "frame"), "space", None),
        P(("dp", "frame"), "space", None),
        P("space", None),
        P("space", None),
        P("space", None),
        P("space", None),
        P(),
    )
    out_specs = (P(("dp", "frame"), "space", None), P(("dp", "frame"), "space", None))
    return jax.shard_map(local, mesh=mesh, in_specs=in_specs, out_specs=out_specs, check_vma=False)
```

profile of v0, /device:TPU:198, one launch (start us, length us, event | category | flops | bytes accessed | tf_op | source)
XLA Modules:
  0.0 301.4 jit_solution(5994388892875304705)
XLA Ops:
  7.2 1.7 pad_maximum_fusion.3
  9.3 1.0 fusion.55
  11.0 109.4 %all-gather.2.cloned.1.call-done = bf16[768,6144]{1,0:T(8,128)(2,1)} async-done(((bf16[24,6144]{1,0:T(8,128)(2,1)}), bf16[768,6144]{1,0:T(8,128)(2,1)}) %all-gather.2.cloned.1.call-update) | async-done | bytes 9437200 | tf_op jit(solution)/shard_map/all_gather | solution.py:214
  120.4 2.8 convolution_convert_fusion.1
  123.3 4.6 %collective-permute-start.2 = (bf16[128,768]{1,0:T(8,128)(2,1)S(1)}, bf16[128,768]{1,0:T(8,128)(2,1)S(1)}, u32[]{:S(2)}, u32[]{:S(2)}) collective-permute-start(bf16[128,768]{1,0:T(8,128)(2,1)S(1)} %get-tuple-element.27), channel_id=1, source_target_pairs={{0,2},{2,4},{4,6},{6,8},{8,10},{10,12},{12,14},{14,16},{16,18},{18... | collective-permute-start | bytes 589832 | tf_op jit(solution)/shard_map/ppermute | solution.py:20
  127.9 1.9 collective-permute-start.3
  129.9 7.2 %collective-permute-start = (bf16[128,768]{1,0:T(8,128)(2,1)S(1)}, bf16[128,768]{1,0:T(8,128)(2,1)S(1)}, u32[]{:S(2)}, u32[]{:S(2)}) collective-permute-start(bf16[128,768]{1,0:T(8,128)(2,1)S(1)} %get-tuple-element.28), channel_id=1, source_target_pairs={{0,2},{2,4},{4,6},{6,8},{8,10},{10,12},{12,14},{14,16},{16,18},{18... | collective-permute-start | bytes 589832 | tf_op jit(solution)/shard_map/ppermute | solution.py:20
  137.1 1.9 collective-permute-start.1
  139.8 1.8 fusion.43
  142.5 1.8 reduce.19
  145.0 6.7 %all-to-all-start.2 = ((bf16[8,2,6144]{2,1,0:T(2,128)(2,1)}), bf16[8,2,6144]{2,1,0:T(2,128)(2,1)S(1)}, u32[]{:S(2)}, u32[]{:S(2)}) async-start(bf16[8,2,6144]{2,1,0:T(2,128)(2,1)} %reshape.405), calls=%async_computation.2 | async-start | bytes 393216 | tf_op jit(solution)/shard_map/all_to_all | solution.py:198
  158.7 1.7 multiply_reduce_fusion.2
  160.4 2.7 fusion
  164.1 4.3 %reduce.20 = bf16[128,2304]{1,0:T(8,128)(2,1)S(1)} reduce(bf16[128,1,2304]{2,1,0:T(2,128)(2,1)S(1)} %bitcast.286, bf16[]{:T(256)} %broadcast.211), dimensions={1}, to_apply=%bitcast.285.reduce_sub_computation | reduce | bytes 1179650
  169.3 7.2 %all-to-all-start = ((bf16[8,2,18432]{2,1,0:T(2,128)(2,1)}), bf16[8,2,18432]{2,1,0:T(2,128)(2,1)S(1)}, u32[]{:S(2)}, u32[]{:S(2)}) async-start(bf16[8,2,18432]{2,1,0:T(2,128)(2,1)} %reshape.403), calls=%async_computation | async-start | bytes 1179648 | tf_op jit(solution)/shard_map/all_to_all | solution.py:198
  177.1 1.1 fusion.94
  178.2 1.1 fusion.96
  179.5 1.1 bitcast_reduce_fusion
  180.9 1.1 bitcast_convert_fusion
  182.0 11.6 %all-to-all-done = bf16[8,2,18432]{2,1,0:T(2,128)(2,1)S(1)} async-done(((bf16[8,2,18432]{2,1,0:T(2,128)(2,1)}), bf16[8,2,18432]{2,1,0:T(2,128)(2,1)S(1)}, u32[]{:S(2)}, u32[]{:S(2)}) %all-to-all-start) | async-done | bytes 589856 | tf_op jit(solution)/shard_map/all_to_all | solution.py:198
  195.4 1.3 fusion.8
  197.5 1.1 fusion.67
  198.6 3.4 %multiply_reduce_fusion = (f32[16,12,8]{2,1,0:T(8,128)S(1)}, bf16[16,12,64,8]{2,3,1,0:T(8,128)(2,1)}) fusion(f32[16,12,8,64]{3,1,0,2:T(8,128)} %bitcast_convert_fusion, f32[16,12,8,8]{2,3,1,0:T(8,128)} %copy-done.54, bf16[8,16,12,64]{3,2,1,0:T(8,128)(2,1)S(1)} %reshape.347), kind=kOutput, calls=%fused_computation.101 | convolution fusion | flops 1990663 | bytes 841728 | tf_op jit(solution)/shard_map/phfg,gphd->fphd/dot_general | solution.py:143
  202.0 1.7 fusion.10
  203.8 1.2 fusion.15
  205.4 2.0 fusion.13
  210.0 3.4 %all-to-all-start.1 = ((bf16[8,16,768]{2,1,0:T(8,128)(2,1)}), bf16[8,16,768]{2,1,0:T(8,128)(2,1)S(1)}, u32[]{:S(2)}, u32[]{:S(2)}) async-start(bf16[8,16,768]{2,1,0:T(8,128)(2,1)} %reshape.350), calls=%async_computation.1 | async-start | bytes 393216 | tf_op jit(solution)/shard_map/all_to_all | solution.py:202
  214.2 8.8 %all-to-all-done.1 = bf16[8,16,768]{2,1,0:T(8,128)(2,1)S(1)} async-done(((bf16[8,16,768]{2,1,0:T(8,128)(2,1)}), bf16[8,16,768]{2,1,0:T(8,128)(2,1)S(1)}, u32[]{:S(2)}, u32[]{:S(2)}) %all-to-all-start.1) | async-done | bytes 196640 | tf_op jit(solution)/shard_map/all_to_all | solution.py:202
  223.0 3.8 %all-to-all-start.3 = ((bf16[8,16,2304]{2,1,0:T(8,128)(2,1)}), bf16[8,16,2304]{2,1,0:T(8,128)(2,1)S(1)}, u32[]{:S(2)}, u32[]{:S(2)}) async-start(bf16[8,16,2304]{2,1,0:T(8,128)(2,1)} %pad_maximum_fusion.2), calls=%async_computation.3 | async-start | bytes 1179648 | tf_op jit(solution)/shard_map/all_to_all | solution.py:202
  228.4 1.1 fusion.88
  229.5 1.1 fusion.86
  230.6 2.3 fusion.44
  232.9 8.2 %all-to-all-done.3 = bf16[8,16,2304]{2,1,0:T(8,128)(2,1)S(1)} async-done(((bf16[8,16,2304]{2,1,0:T(8,128)(2,1)}), bf16[8,16,2304]{2,1,0:T(8,128)(2,1)S(1)}, u32[]{:S(2)}, u32[]{:S(2)}) %all-to-all-start.3) | async-done | bytes 589856 | tf_op jit(solution)/shard_map/all_to_all | solution.py:202
  241.1 3.4 %multiply_reduce_fusion.1 = (f32[128]{0:T(128)S(1)}, f32[128,768]{1,0:T(8,128)S(1)}) fusion(f32[128,768]{1,0:T(8,128)S(1)} %get-tuple-element.40, bf16[128,2304]{1,0:T(8,128)(2,1)S(1)} %bitcast.315, bf16[768,6144]{1,0:T(8,128)(2,1)} %all-gather.2.cloned.1.call-done), kind=kOutput, calls=%fused_computation.120 | convolution fusion | flops 453181312 | bytes 4915712 | tf_op jit(solution)/shard_map/dot_general | solution.py:257
  244.7 1.8 convolution_convert_fusion.4
  247.3 2.1 fusion.98
  250.3 2.1 fusion.101
  253.2 1.4 fusion.104
  255.5 1.4 fusion.107
  257.7 1.5 fusion.110
  260.1 1.4 fusion.113
  263.0 6.7 %collective-permute-start.6 = (bf16[128,768]{0,1:T(8,128)(2,1)S(1)}, bf16[128,768]{0,1:T(8,128)(2,1)S(1)}, u32[]{:S(2)}, u32[]{:S(2)}) collective-permute-start(bf16[128,768]{0,1:T(8,128)(2,1)S(1)} %get-tuple-element.2), channel_id=1, source_target_pairs={{0,2},{2,4},{4,6},{6,8},{8,10},{10,12},{12,14},{14,16},{16,18},{18... | collective-permute-start | bytes 589832 | tf_op jit(solution)/shard_map/ppermute | solution.py:20
  269.7 1.9 collective-permute-start.7
  271.9 7.2 %collective-permute-start.4 = (bf16[128,768]{0,1:T(8,128)(2,1)S(1)}, bf16[128,768]{0,1:T(8,128)(2,1)S(1)}, u32[]{:S(2)}, u32[]{:S(2)}) collective-permute-start(bf16[128,768]{0,1:T(8,128)(2,1)S(1)} %get-tuple-element.4), channel_id=1, source_target_pairs={{0,2},{2,4},{4,6},{6,8},{8,10},{10,12},{12,14},{14,16},{16,18},{18... | collective-permute-start | bytes 589832 | tf_op jit(solution)/shard_map/ppermute | solution.py:20
  279.1 1.9 collective-permute-start.5
  281.1 1.1 collective-permute-done.4
  282.3 7.7 %collective-permute-done.5 = bf16[128,768]{0,1:T(8,128)(2,1)S(1)} collective-permute-done((bf16[128,768]{0,1:T(8,128)(2,1)S(1)}, bf16[128,768]{0,1:T(8,128)(2,1)S(1)}, u32[]{:S(2)}, u32[]{:S(2)}) %collective-permute-start.5) | collective-permute-done | bytes 196640 | tf_op jit(solution)/shard_map/ppermute | solution.py:22
  290.2 3.4 %fusion.61 = (f32[128]{0:T(128)S(1)}, f32[128,768]{1,0:T(8,128)S(1)}) fusion(bf16[1,128,768]{2,1,0:T(8,128)(2,1)S(1)} %copy-done.1, bf16[128,2304]{0,1:T(8,128)(2,1)S(1)} %fusion.77, bf16[768,6144]{1,0:T(8,128)(2,1)} %all-gather.2.cloned.1.call-done), kind=kOutput, calls=%fused_computation.112 | convolution fusion | flops 453279616 | bytes 4719104 | tf_op jit(solution)/shard_map/dot_general | solution.py:287
  (252 shorter events, 28.3 us)
Async XLA Ops:
  7.2 1.8 copy-start
  7.2 113.2 %all-gather.2.cloned.1.call-start = ((), (), s32[]{:S(2)}) async-start(), calls=%async_computation.4 | async-start | bytes 9732096 | tf_op jit(solution)/shard_map/all_gather | solution.py:214
  11.0 109.4 %copy-start.52 = (f32[128]{0:T(128)}, f32[128]{0:T(128)S(1)}, u32[]{:S(2)}) copy-start(f32[128]{0:T(128)S(1)} %get-tuple-element.36) | copy-start | bytes 1540
  123.2 16.6 %copy-start.34 = (bf16[1,128,768]{2,1,0:T(8,128)(2,1)S(1)}, bf16[1,128,768]{2,1,0:T(8,128)(2,1)}, u32[]{:S(2)}) copy-start(bf16[1,128,768]{2,1,0:T(8,128)(2,1)} %param.8) | copy-start | bytes 589828
  123.3 28.5 %collective-permute-start.2 = (bf16[128,768]{1,0:T(8,128)(2,1)S(1)}, bf16[128,768]{1,0:T(8,128)(2,1)S(1)}, u32[]{:S(2)}, u32[]{:S(2)}) collective-permute-start(bf16[128,768]{1,0:T(8,128)(2,1)S(1)} %get-tuple-element.27), channel_id=1, source_target_pairs={{0,2},{2,4},{4,6},{6,8},{8,10},{10,12},{12,14},{14,16},{16,18},{18... | collective-permute-start | bytes 589832 | tf_op jit(solution)/shard_map/ppermute | solution.py:20
  127.9 23.9 %collective-permute-start.3 = (bf16[128,768]{1,0:T(8,128)(2,1)S(1)}, bf16[128,768]{1,0:T(8,128)(2,1)S(1)}, u32[]{:S(2)}, u32[]{:S(2)}) collective-permute-start(bf16[128,768]{1,0:T(8,128)(2,1)S(1)} %get-tuple-element.27), channel_id=1, source_target_pairs={{2,0},{4,2},{6,4},{8,6},{10,8},{12,10},{14,12},{16,14},{18,16},{20... | collective-permute-start | bytes 589832 | tf_op jit(solution)/shard_map/ppermute | solution.py:22
  129.9 22.2 %collective-permute-start = (bf16[128,768]{1,0:T(8,128)(2,1)S(1)}, bf16[128,768]{1,0:T(8,128)(2,1)S(1)}, u32[]{:S(2)}, u32[]{:S(2)}) collective-permute-start(bf16[128,768]{1,0:T(8,128)(2,1)S(1)} %get-tuple-element.28), channel_id=1, source_target_pairs={{0,2},{2,4},{4,6},{6,8},{8,10},{10,12},{12,14},{14,16},{16,18},{18... | collective-permute-start | bytes 589832 | tf_op jit(solution)/shard_map/ppermute | solution.py:20
  137.1 15.0 %collective-permute-start.1 = (bf16[128,768]{1,0:T(8,128)(2,1)S(1)}, bf16[128,768]{1,0:T(8,128)(2,1)S(1)}, u32[]{:S(2)}, u32[]{:S(2)}) collective-permute-start(bf16[128,768]{1,0:T(8,128)(2,1)S(1)} %get-tuple-element.28), channel_id=1, source_target_pairs={{2,0},{4,2},{6,4},{8,6},{10,8},{12,10},{14,12},{16,14},{18,16},{20... | collective-permute-start | bytes 589832 | tf_op jit(solution)/shard_map/ppermute | solution.py:22
  139.4 16.0 %copy-start.26 = (bf16[128,128]{0,1:T(8,128)(2,1)}, bf16[128,128]{0,1:T(8,128)(2,1)S(1)}, u32[]{:S(2)}) copy-start(bf16[128,128]{0,1:T(8,128)(2,1)S(1)} %copy.191) | copy-start | bytes 98308
  139.5 16.5 %copy-start.28 = (bf16[128,128]{0,1:T(8,128)(2,1)}, bf16[128,128]{0,1:T(8,128)(2,1)S(1)}, u32[]{:S(2)}) copy-start(bf16[128,128]{0,1:T(8,128)(2,1)S(1)} %copy.194) | copy-start | bytes 98308
  139.7 17.0 %copy-start.30 = (bf16[128,128]{0,1:T(8,128)(2,1)}, bf16[128,128]{0,1:T(8,128)(2,1)S(1)}, u32[]{:S(2)}) copy-start(bf16[128,128]{0,1:T(8,128)(2,1)S(1)} %copy.197) | copy-start | bytes 98308
  139.8 17.8 %copy-start.32 = (bf16[128,128]{0,1:T(8,128)(2,1)}, bf16[128,128]{0,1:T(8,128)(2,1)S(1)}, u32[]{:S(2)}) copy-start(bf16[128,128]{0,1:T(8,128)(2,1)S(1)} %copy.200) | copy-start | bytes 98308
  145.0 24.3 %all-to-all-start.2 = ((bf16[8,2,6144]{2,1,0:T(2,128)(2,1)}), bf16[8,2,6144]{2,1,0:T(2,128)(2,1)S(1)}, u32[]{:S(2)}, u32[]{:S(2)}) async-start(bf16[8,2,6144]{2,1,0:T(2,128)(2,1)} %reshape.405), calls=%async_computation.2 | async-start | bytes 393216 | tf_op jit(solution)/shard_map/all_to_all | solution.py:198
  152.4 2.7 copy-start.16
  154.2 2.1 copy-start.20
  154.5 2.5 copy-start.22
  154.8 3.1 %copy-start.24 = (bf16[384,128]{0,1:T(8,128)(2,1)}, bf16[384,128]{0,1:T(8,128)(2,1)S(1)}, u32[]{:S(2)}) copy-start(bf16[384,128]{0,1:T(8,128)(2,1)S(1)} %copy.199) | copy-start | bytes 294916
  157.6 2.8 copy-start.47
  158.2 4.9 %copy-start.49 = (bf16[2,64,128]{2,1,0:T(8,128)(2,1)}, bf16[2,64,128]{2,1,0:T(8,128)(2,1)S(1)}, u32[]{:S(2)}) copy-start(bf16[2,64,128]{2,1,0:T(8,128)(2,1)S(1)} %convolution_convert_fusion.6) | copy-start | bytes 98308
  169.3 24.3 %all-to-all-start = ((bf16[8,2,18432]{2,1,0:T(2,128)(2,1)}), bf16[8,2,18432]{2,1,0:T(2,128)(2,1)S(1)}, u32[]{:S(2)}, u32[]{:S(2)}) async-start(bf16[8,2,18432]{2,1,0:T(2,128)(2,1)} %reshape.403), calls=%async_computation | async-start | bytes 1179648 | tf_op jit(solution)/shard_map/all_to_all | solution.py:198
  205.4 2.0 copy-start.2
  210.0 13.1 %all-to-all-start.1 = ((bf16[8,16,768]{2,1,0:T(8,128)(2,1)}), bf16[8,16,768]{2,1,0:T(8,128)(2,1)S(1)}, u32[]{:S(2)}, u32[]{:S(2)}) async-start(bf16[8,16,768]{2,1,0:T(8,128)(2,1)} %reshape.350), calls=%async_computation.1 | async-start | bytes 393216 | tf_op jit(solution)/shard_map/all_to_all | solution.py:202
  213.4 13.5 %copy-start.27 = (bf16[128,128]{0,1:T(8,128)(2,1)S(1)}, bf16[128,128]{0,1:T(8,128)(2,1)}, u32[]{:S(2)}) copy-start(bf16[128,128]{0,1:T(8,128)(2,1)} %copy-done.26) | copy-start | bytes 98308
  223.0 18.1 %all-to-all-start.3 = ((bf16[8,16,2304]{2,1,0:T(8,128)(2,1)}), bf16[8,16,2304]{2,1,0:T(8,128)(2,1)S(1)}, u32[]{:S(2)}, u32[]{:S(2)}) async-start(bf16[8,16,2304]{2,1,0:T(8,128)(2,1)} %pad_maximum_fusion.2), calls=%async_computation.3 | async-start | bytes 1179648 | tf_op jit(solution)/shard_map/all_to_all | solution.py:202
  241.1 3.4 %copy-start.35 = (bf16[1,128,768]{2,1,0:T(8,128)(2,1)S(1)}, bf16[1,128,768]{2,1,0:T(8,128)(2,1)}, u32[]{:S(2)}) copy-start(bf16[1,128,768]{2,1,0:T(8,128)(2,1)} %param.8) | copy-start | bytes 589828
  244.7 2.6 copy-start.50
  246.5 2.9 copy-start.13
  246.5 2.9 copy-start.25
  247.3 2.9 copy-start.48
  249.7 2.6 copy-start.12
  249.7 2.6 copy-start.23
  250.3 2.9 copy-start.46
  252.6 2.0 copy-start.21
  253.2 2.2 copy-start.44
  254.9 2.0 copy-start.19
  255.5 2.2 copy-start.42
  257.1 2.1 copy-start.11
  257.1 2.1 copy-start.17
  257.7 2.2 copy-start.38
  257.7 2.3 copy-start.40
  259.5 2.0 copy-start.10
  259.5 2.0 copy-start.15
  263.0 27.1 %collective-permute-start.6 = (bf16[128,768]{0,1:T(8,128)(2,1)S(1)}, bf16[128,768]{0,1:T(8,128)(2,1)S(1)}, u32[]{:S(2)}, u32[]{:S(2)}) collective-permute-start(bf16[128,768]{0,1:T(8,128)(2,1)S(1)} %get-tuple-element.2), channel_id=1, source_target_pairs={{0,2},{2,4},{4,6},{6,8},{8,10},{10,12},{12,14},{14,16},{16,18},{18... | collective-permute-start | bytes 589832 | tf_op jit(solution)/shard_map/ppermute | solution.py:20
  269.7 20.4 %collective-permute-start.7 = (bf16[128,768]{0,1:T(8,128)(2,1)S(1)}, bf16[128,768]{0,1:T(8,128)(2,1)S(1)}, u32[]{:S(2)}, u32[]{:S(2)}) collective-permute-start(bf16[128,768]{0,1:T(8,128)(2,1)S(1)} %get-tuple-element.3), channel_id=1, source_target_pairs={{2,0},{4,2},{6,4},{8,6},{10,8},{12,10},{14,12},{16,14},{18,16},{20... | collective-permute-start | bytes 589832 | tf_op jit(solution)/shard_map/ppermute | solution.py:22
  271.9 10.4 %collective-permute-start.4 = (bf16[128,768]{0,1:T(8,128)(2,1)S(1)}, bf16[128,768]{0,1:T(8,128)(2,1)S(1)}, u32[]{:S(2)}, u32[]{:S(2)}) collective-permute-start(bf16[128,768]{0,1:T(8,128)(2,1)S(1)} %get-tuple-element.4), channel_id=1, source_target_pairs={{0,2},{2,4},{4,6},{6,8},{8,10},{10,12},{12,14},{14,16},{16,18},{18... | collective-permute-start | bytes 589832 | tf_op jit(solution)/shard_map/ppermute | solution.py:20
  279.1 10.9 %collective-permute-start.5 = (bf16[128,768]{0,1:T(8,128)(2,1)S(1)}, bf16[128,768]{0,1:T(8,128)(2,1)S(1)}, u32[]{:S(2)}, u32[]{:S(2)}) collective-permute-start(bf16[128,768]{0,1:T(8,128)(2,1)S(1)} %get-tuple-element.5), channel_id=1, source_target_pairs={{2,0},{4,2},{6,4},{8,6},{10,8},{12,10},{14,12},{16,14},{18,16},{20... | collective-permute-start | bytes 589832 | tf_op jit(solution)/shard_map/ppermute | solution.py:22
  290.2 3.4 %copy-start.51 = (f32[128]{0:T(128)S(1)}, f32[128]{0:T(128)}, u32[]{:S(2)}) copy-start(f32[128]{0:T(128)} %get-tuple-element.35) | copy-start | bytes 1540
  290.2 3.4 %copy-start.53 = (f32[128]{0:T(128)S(1)}, f32[128]{0:T(128)}, u32[]{:S(2)}) copy-start(f32[128]{0:T(128)} %copy-done.52) | copy-start | bytes 1540
  (20 other events, 20.1 us)
Sparse Core Ops, SparseCore 0:
  11.2 109.1 all-gather.1
where the time goes:
time: 303 us; the launch traced here: 301 us
  waiting for transfers between devices  147 us (49%)
  starting transfers between devices  54.6 us (18%)
  matrix products  52 us (17%)
  local copies, waits for them, and re-layouts  17.4 us (6%)
  between operations  15.7 us (5%)
  other arithmetic  14.7 us (5%)
    all_gather x1, waiting for transfers between devices, local(): all_weights = lax.all_gather(weight_rows, 'space', axis=0, tiled=True)  109 us
    ppermute x4, starting transfers between devices, padded(): lax.ppermute(tail, axis, [(i, (i + 1) % count) for i in range(ends)])  25.8 us
    all_to_all x2, waiting for transfers between devices, to_space(): lax.all_to_all(frame_rows, 'frame', split_axis=0, concat_axis=1, tiled=True)  17 us
    all_to_all x2, starting transfers between devices, to_frames(): lax.all_to_all(local_rows[None], 'frame', split_axis=1, concat_axis=0, ti...  13.9 us
    all_to_all x2, waiting for transfers between devices, to_frames(): lax.all_to_all(local_rows[None], 'frame', split_axis=1, concat_axis=0, ti...  11.6 us
    dot_general x6, matrix products, space_back(): jnp.einsum('gst,sgh->tgh', probability, grad_part, preferred_element_type...  9.81 us
    ppermute x4, waiting for transfers between devices, padded(): lax.ppermute(head, axis, [((i + 1) % count, i) for i in range(ends)])  7.72 us
    ppermute x4, starting transfers between devices, padded(): lax.ppermute(head, axis, [((i + 1) % count, i) for i in range(ends)])  7.68 us
  transfers between devices with their start and end apart: 13, of which 6 were waited for; matrix products, arithmetic and copies ran while one was open for 12% of the time, Pallas kernels for 0%

commit v1 on v0

--- a/solution.py
+++ b/solution.py
@@ -211,7 +211,9 @@
     grad_out = cotangent[0]
     shard, feature_count = local_in.shape
     weight_rows = jnp.concatenate([w_qkv_space, w_out_space, w_qkv_time, w_out_time], axis=1)
-    all_weights = lax.all_gather(weight_rows, "space", axis=0, tiled=True)
+    all_weights = jnp.concatenate(
+        lax.all_to_all(jnp.stack([weight_rows] * lax.axis_size("space")), "space", 0, 0), axis=0
+    )
     widths = [w_qkv_space.shape[1], w_out_space.shape[1], w_qkv_time.shape[1], w_out_time.shape[1]]
     bounds = [0]
     for width in widths:

time: 303 us -> 417 us (1.38)
  waiting for transfers between devices: 147 us -> 262 us
  between operations: 15.7 us -> 2.36 us
  starting transfers between devices: 54.6 us -> 63.2 us
    all_to_all x0 -> x1, waiting for transfers between devices: none -> 223 us  [local(): lax.all_to_all(jnp.stack([weight_rows] * lax.axis_size('space')), 'space'...]
    all_gather x1 -> x0, waiting for transfers between devices: 109 us -> none  [local(): all_weights = lax.all_gather(weight_rows, 'space', axis=0, tiled=True)]
    all_to_all x0 -> x1, starting transfers between devices: none -> 10.9 us  [local(): lax.all_to_all(jnp.stack([weight_rows] * lax.axis_size('space')), 'space'...]
    another operation x0 -> x1, local copies, waits for them, and re-layouts: none -> 4.82 us  [local(): jnp.stack([weight_rows] * lax.axis_size('space'))]
    ppermute x4, starting transfers between devices: 25.8 us -> 21.1 us  [padded(): lax.ppermute(tail, axis, [(i, (i + 1) % count) for i in range(ends)])]
  transfers between devices with their start and end apart: 13 -> 13, of which waited for: 6 -> 6; matrix products, arithmetic and copies ran while one was open for 12% -> 8% of each run, Pallas kernels for 0% -> 0%
where the time goes in v1:
time: 417 us; the launch traced here: 416 us
  waiting for transfers between devices  262 us (63%)
  starting transfers between devices  63.2 us (15%)
  matrix products  54.2 us (13%)
  local copies, waits for them, and re-layouts  21 us (5%)
  other arithmetic  13.2 us (3%)
    all_to_all x1, waiting for transfers between devices, local(): lax.all_to_all(jnp.stack([weight_rows] * lax.axis_size('space')), 'space'...  223 us
    ppermute x4, starting transfers between devices, padded(): lax.ppermute(tail, axis, [(i, (i + 1) % count) for i in range(ends)])  21.1 us
    all_to_all x2, waiting for transfers between devices, to_space(): lax.all_to_all(frame_rows, 'frame', split_axis=0, concat_axis=1, tiled=True)  18.4 us
    all_to_all x2, starting transfers between devices, to_frames(): lax.all_to_all(local_rows[None], 'frame', split_axis=1, concat_axis=0, ti...  14.3 us
    all_to_all x2, waiting for transfers between devices, to_frames(): lax.all_to_all(local_rows[None], 'frame', split_axis=1, concat_axis=0, ti...  12 us
    all_to_all x1, starting transfers between devices, local(): lax.all_to_all(jnp.stack([weight_rows] * lax.axis_size('space')), 'space'...  10.9 us
    dot_general x6, matrix products, space_back(): jnp.einsum('gst,sgh->tgh', probability, grad_part, preferred_element_type...  9.78 us
    ppermute x4, starting transfers between devices, padded(): lax.ppermute(head, axis, [((i + 1) % count, i) for i in range(ends)])  9.68 us
  transfers between devices with their start and end apart: 13, of which 6 were waited for; matrix products, arithmetic and copies ran while one was open for 8% of the time, Pallas kernels for 0%

profile of v1, /device:TPU:198, one launch (start us, length us, event | category | flops | bytes accessed | tf_op | source)
XLA Modules:
  0.0 415.8 jit_solution(6289985336670856458)
XLA Ops:
  0.6 1.0 pad_maximum_fusion.3
  1.7 4.8 %stack.2 = bf16[32,24,6144]{2,1,0:T(8,128)(2,1)} broadcast(bf16[24,6144]{1,0:T(8,128)(2,1)S(1)} %pad_maximum_fusion.3), dimensions={1,2} | broadcast | bytes 9732096 | tf_op jit(solution)/shard_map/stack | solution.py:215
  6.5 10.9 %all-to-all-start = ((bf16[32,24,6144]{2,1,0:T(8,128)(2,1)}), bf16[32,24,6144]{2,1,0:T(8,128)(2,1)}, u32[]{:S(2)}, u32[]{:S(2)}) async-start(bf16[32,24,6144]{2,1,0:T(8,128)(2,1)} %stack.2), calls=%async_computation | async-start | bytes 18874368 | tf_op jit(solution)/shard_map/all_to_all | solution.py:215
  18.4 222.7 %all-to-all-done = bf16[32,24,6144]{2,1,0:T(8,128)(2,1)} async-done(((bf16[32,24,6144]{2,1,0:T(8,128)(2,1)}), bf16[32,24,6144]{2,1,0:T(8,128)(2,1)}, u32[]{:S(2)}, u32[]{:S(2)}) %all-to-all-start) | async-done | bytes 9437216 | tf_op jit(solution)/shard_map/all_to_all | solution.py:215
  241.1 2.7 convolution_convert_fusion.1
  243.8 2.1 collective-permute-start.2
  245.9 3.9 collective-permute-start.3
  249.9 5.2 %collective-permute-start = (bf16[128,768]{1,0:T(8,128)(2,1)S(1)}, bf16[128,768]{1,0:T(8,128)(2,1)S(1)}, u32[]{:S(2)}, u32[]{:S(2)}) collective-permute-start(bf16[128,768]{1,0:T(8,128)(2,1)S(1)} %get-tuple-element.28), channel_id=1, source_target_pairs={{0,2},{2,4},{4,6},{6,8},{8,10},{10,12},{12,14},{14,16},{16,18},{18... | collective-permute-start | bytes 589832 | tf_op jit(solution)/shard_map/ppermute | solution.py:20
  255.1 1.9 collective-permute-start.1
  257.8 1.8 fusion.43
  260.6 1.8 reduce.19
  263.2 7.1 %all-to-all-start.3 = ((bf16[8,2,6144]{2,1,0:T(2,128)(2,1)}), bf16[8,2,6144]{2,1,0:T(2,128)(2,1)S(1)}, u32[]{:S(2)}, u32[]{:S(2)}) async-start(bf16[8,2,6144]{2,1,0:T(2,128)(2,1)} %reshape.411), calls=%async_computation.3 | async-start | bytes 393216 | tf_op jit(solution)/shard_map/all_to_all | solution.py:198
  277.4 1.7 multiply_reduce_fusion.2
  279.2 2.7 fusion
  282.8 4.3 %reduce.20 = bf16[128,2304]{1,0:T(8,128)(2,1)S(1)} reduce(bf16[128,1,2304]{2,1,0:T(2,128)(2,1)S(1)} %bitcast.287, bf16[]{:T(256)} %broadcast.213), dimensions={1}, to_apply=%bitcast.286.reduce_sub_computation | reduce | bytes 1179650
  288.1 7.2 %all-to-all-start.1 = ((bf16[8,2,18432]{2,1,0:T(2,128)(2,1)}), bf16[8,2,18432]{2,1,0:T(2,128)(2,1)S(1)}, u32[]{:S(2)}, u32[]{:S(2)}) async-start(bf16[8,2,18432]{2,1,0:T(2,128)(2,1)} %reshape.409), calls=%async_computation.1 | async-start | bytes 1179648 | tf_op jit(solution)/shard_map/all_to_all | solution.py:198
  295.9 1.1 fusion.86
  297.0 1.1 fusion.88
  298.3 1.1 bitcast_reduce_fusion
  299.8 1.1 bitcast_convert_fusion
  300.8 12.0 %all-to-all-done.1 = bf16[8,2,18432]{2,1,0:T(2,128)(2,1)S(1)} async-done(((bf16[8,2,18432]{2,1,0:T(2,128)(2,1)}), bf16[8,2,18432]{2,1,0:T(2,128)(2,1)S(1)}, u32[]{:S(2)}, u32[]{:S(2)}) %all-to-all-start.1) | async-done | bytes 589856 | tf_op jit(solution)/shard_map/all_to_all | solution.py:198
  314.5 1.3 fusion.8
  316.7 1.1 fusion.67
  317.8 3.4 multiply_reduce_fusion
  321.2 1.7 fusion.10
  323.8 2.7 fusion.13
  329.1 3.4 all-to-all-start.2
  333.4 8.8 %all-to-all-done.2 = bf16[8,16,768]{2,1,0:T(8,128)(2,1)S(1)} async-done(((bf16[8,16,768]{2,1,0:T(8,128)(2,1)}), bf16[8,16,768]{2,1,0:T(8,128)(2,1)S(1)}, u32[]{:S(2)}, u32[]{:S(2)}) %all-to-all-start.2) | async-done | bytes 196640 | tf_op jit(solution)/shard_map/all_to_all | solution.py:202
  342.2 3.8 all-to-all-start.4
  346.0 1.1 fusion.90
  347.1 1.1 fusion.92
  349.0 2.3 fusion.44
  351.2 9.6 %all-to-all-done.4 = bf16[8,16,2304]{2,1,0:T(8,128)(2,1)S(1)} async-done(((bf16[8,16,2304]{2,1,0:T(8,128)(2,1)}), bf16[8,16,2304]{2,1,0:T(8,128)(2,1)S(1)}, u32[]{:S(2)}, u32[]{:S(2)}) %all-to-all-start.4) | async-done | bytes 589856 | tf_op jit(solution)/shard_map/all_to_all | solution.py:202
  360.8 3.4 multiply_reduce_fusion.1
  364.4 1.8 convolution_convert_fusion.4
  366.5 1.4 fusion.98
  369.3 2.1 fusion.101
  372.9 1.4 fusion.104
  375.7 2.1 fusion.107
  379.2 1.5 fusion.110
  381.6 1.4 fusion.113
  384.3 6.6 %collective-permute-start.6 = (bf16[128,768]{0,1:T(8,128)(2,1)S(1)}, bf16[128,768]{0,1:T(8,128)(2,1)S(1)}, u32[]{:S(2)}, u32[]{:S(2)}) collective-permute-start(bf16[128,768]{0,1:T(8,128)(2,1)S(1)} %get-tuple-element.2), channel_id=1, source_target_pairs={{0,2},{2,4},{4,6},{6,8},{8,10},{10,12},{12,14},{14,16},{16,18},{18... | collective-permute-start | bytes 589832 | tf_op jit(solution)/shard_map/ppermute | solution.py:20
  390.9 1.9 collective-permute-start.7
  393.2 7.2 %collective-permute-start.4 = (bf16[128,768]{0,1:T(8,128)(2,1)S(1)}, bf16[128,768]{0,1:T(8,128)(2,1)S(1)}, u32[]{:S(2)}, u32[]{:S(2)}) collective-permute-start(bf16[128,768]{0,1:T(8,128)(2,1)S(1)} %get-tuple-element.4), channel_id=1, source_target_pairs={{0,2},{2,4},{4,6},{6,8},{8,10},{10,12},{12,14},{14,16},{16,18},{18... | collective-permute-start | bytes 589832 | tf_op jit(solution)/shard_map/ppermute | solution.py:20
  400.4 1.9 collective-permute-start.5
  402.5 1.1 collective-permute-done.4
  403.6 7.7 %collective-permute-done.5 = bf16[128,768]{0,1:T(8,128)(2,1)S(1)} collective-permute-done((bf16[128,768]{0,1:T(8,128)(2,1)S(1)}, bf16[128,768]{0,1:T(8,128)(2,1)S(1)}, u32[]{:S(2)}, u32[]{:S(2)}) %collective-permute-start.5) | collective-permute-done | bytes 196640 | tf_op jit(solution)/shard_map/ppermute | solution.py:22
  411.5 3.4 fusion.61
  (262 shorter events, 30.0 us)
Async XLA Ops:
  0.6 16.7 %copy-start = (s32[32,4]{0,1:T(4,128)S(1)}, s32[32,4]{0,1:T(4,128)}, u32[]{:S(2)}) copy-start(s32[32,4]{0,1:T(4,128)} %param.13) | copy-start | bytes 1540
  6.5 11.2 %copy-start.1 = (bf16[1,128,768]{2,1,0:T(8,128)(2,1)S(1)}, bf16[1,128,768]{2,1,0:T(8,128)(2,1)}, u32[]{:S(2)}) copy-start(bf16[1,128,768]{2,1,0:T(8,128)(2,1)} %param.7) | copy-start | bytes 589828
  6.5 234.6 %all-to-all-start = ((bf16[32,24,6144]{2,1,0:T(8,128)(2,1)}), bf16[32,24,6144]{2,1,0:T(8,128)(2,1)}, u32[]{:S(2)}, u32[]{:S(2)}) async-start(bf16[32,24,6144]{2,1,0:T(8,128)(2,1)} %stack.2), calls=%async_computation | async-start | bytes 18874368 | tf_op jit(solution)/shard_map/all_to_all | solution.py:215
  18.4 222.7 %copy-start.57 = (f32[128]{0:T(128)}, f32[128]{0:T(128)S(1)}, u32[]{:S(2)}) copy-start(f32[128]{0:T(128)S(1)} %get-tuple-element.36) | copy-start | bytes 1540
  243.8 14.0 %copy-start.36 = (bf16[1,128,768]{2,1,0:T(8,128)(2,1)S(1)}, bf16[1,128,768]{2,1,0:T(8,128)(2,1)}, u32[]{:S(2)}) copy-start(bf16[1,128,768]{2,1,0:T(8,128)(2,1)} %param.8) | copy-start | bytes 589828
  243.8 26.4 %collective-permute-start.2 = (bf16[128,768]{1,0:T(8,128)(2,1)S(1)}, bf16[128,768]{1,0:T(8,128)(2,1)S(1)}, u32[]{:S(2)}, u32[]{:S(2)}) collective-permute-start(bf16[128,768]{1,0:T(8,128)(2,1)S(1)} %get-tuple-element.27), channel_id=1, source_target_pairs={{0,2},{2,4},{4,6},{6,8},{8,10},{10,12},{12,14},{14,16},{16,18},{18... | collective-permute-start | bytes 589832 | tf_op jit(solution)/shard_map/ppermute | solution.py:20
  245.9 24.4 %collective-permute-start.3 = (bf16[128,768]{1,0:T(8,128)(2,1)S(1)}, bf16[128,768]{1,0:T(8,128)(2,1)S(1)}, u32[]{:S(2)}, u32[]{:S(2)}) collective-permute-start(bf16[128,768]{1,0:T(8,128)(2,1)S(1)} %get-tuple-element.27), channel_id=1, source_target_pairs={{2,0},{4,2},{6,4},{8,6},{10,8},{12,10},{14,12},{16,14},{18,16},{20... | collective-permute-start | bytes 589832 | tf_op jit(solution)/shard_map/ppermute | solution.py:22
  249.9 20.7 %collective-permute-start = (bf16[128,768]{1,0:T(8,128)(2,1)S(1)}, bf16[128,768]{1,0:T(8,128)(2,1)S(1)}, u32[]{:S(2)}, u32[]{:S(2)}) collective-permute-start(bf16[128,768]{1,0:T(8,128)(2,1)S(1)} %get-tuple-element.28), channel_id=1, source_target_pairs={{0,2},{2,4},{4,6},{6,8},{8,10},{10,12},{12,14},{14,16},{16,18},{18... | collective-permute-start | bytes 589832 | tf_op jit(solution)/shard_map/ppermute | solution.py:20
  255.1 15.5 %collective-permute-start.1 = (bf16[128,768]{1,0:T(8,128)(2,1)S(1)}, bf16[128,768]{1,0:T(8,128)(2,1)S(1)}, u32[]{:S(2)}, u32[]{:S(2)}) collective-permute-start(bf16[128,768]{1,0:T(8,128)(2,1)S(1)} %get-tuple-element.28), channel_id=1, source_target_pairs={{2,0},{4,2},{6,4},{8,6},{10,8},{12,10},{14,12},{16,14},{18,16},{20... | collective-permute-start | bytes 589832 | tf_op jit(solution)/shard_map/ppermute | solution.py:22
  257.4 17.1 %copy-start.26 = (bf16[128,128]{0,1:T(8,128)(2,1)}, bf16[128,128]{0,1:T(8,128)(2,1)S(1)}, u32[]{:S(2)}) copy-start(bf16[128,128]{0,1:T(8,128)(2,1)S(1)} %copy.191) | copy-start | bytes 98308
  257.5 17.6 %copy-start.28 = (bf16[128,128]{0,1:T(8,128)(2,1)}, bf16[128,128]{0,1:T(8,128)(2,1)S(1)}, u32[]{:S(2)}) copy-start(bf16[128,128]{0,1:T(8,128)(2,1)S(1)} %copy.194) | copy-start | bytes 98308
  257.7 18.1 %copy-start.30 = (bf16[128,128]{0,1:T(8,128)(2,1)}, bf16[128,128]{0,1:T(8,128)(2,1)S(1)}, u32[]{:S(2)}) copy-start(bf16[128,128]{0,1:T(8,128)(2,1)S(1)} %copy.197) | copy-start | bytes 98308
  257.8 18.6 %copy-start.33 = (bf16[128,128]{0,1:T(8,128)(2,1)}, bf16[128,128]{0,1:T(8,128)(2,1)S(1)}, u32[]{:S(2)}) copy-start(bf16[128,128]{0,1:T(8,128)(2,1)S(1)} %copy.200) | copy-start | bytes 98308
  263.2 25.0 %all-to-all-start.3 = ((bf16[8,2,6144]{2,1,0:T(2,128)(2,1)}), bf16[8,2,6144]{2,1,0:T(2,128)(2,1)S(1)}, u32[]{:S(2)}, u32[]{:S(2)}) async-start(bf16[8,2,6144]{2,1,0:T(2,128)(2,1)} %reshape.411), calls=%async_computation.3 | async-start | bytes 393216 | tf_op jit(solution)/shard_map/all_to_all | solution.py:198
  270.9 2.7 copy-start.16
  272.8 2.7 copy-start.20
  273.0 3.0 copy-start.22
  273.3 3.4 copy-start.24
  276.4 2.8 copy-start.52
  277.0 4.9 %copy-start.54 = (bf16[2,64,128]{2,1,0:T(8,128)(2,1)}, bf16[2,64,128]{2,1,0:T(8,128)(2,1)S(1)}, u32[]{:S(2)}) copy-start(bf16[2,64,128]{2,1,0:T(8,128)(2,1)S(1)} %convolution_convert_fusion.6) | copy-start | bytes 98308
  287.2 8.8 %copy-start.34 = (bf16[128,128]{0,1:T(8,128)(2,1)S(1)}, bf16[128,128]{0,1:T(8,128)(2,1)}, u32[]{:S(2)}) copy-start(bf16[128,128]{0,1:T(8,128)(2,1)} %copy-done.33) | copy-start | bytes 98308
  288.1 24.7 %all-to-all-start.1 = ((bf16[8,2,18432]{2,1,0:T(2,128)(2,1)}), bf16[8,2,18432]{2,1,0:T(2,128)(2,1)S(1)}, u32[]{:S(2)}, u32[]{:S(2)}) async-start(bf16[8,2,18432]{2,1,0:T(2,128)(2,1)} %reshape.409), calls=%async_computation.1 | async-start | bytes 1179648 | tf_op jit(solution)/shard_map/all_to_all | solution.py:198
  329.1 13.1 %all-to-all-start.2 = ((bf16[8,16,768]{2,1,0:T(8,128)(2,1)}), bf16[8,16,768]{2,1,0:T(8,128)(2,1)S(1)}, u32[]{:S(2)}, u32[]{:S(2)}) async-start(bf16[8,16,768]{2,1,0:T(8,128)(2,1)} %reshape.356), calls=%async_computation.2 | async-start | bytes 393216 | tf_op jit(solution)/shard_map/all_to_all | solution.py:202
  332.5 13.5 %copy-start.29 = (bf16[128,128]{0,1:T(8,128)(2,1)S(1)}, bf16[128,128]{0,1:T(8,128)(2,1)}, u32[]{:S(2)}) copy-start(bf16[128,128]{0,1:T(8,128)(2,1)} %copy-done.28) | copy-start | bytes 98308
  342.2 18.6 %all-to-all-start.4 = ((bf16[8,16,2304]{2,1,0:T(8,128)(2,1)}), bf16[8,16,2304]{2,1,0:T(8,128)(2,1)S(1)}, u32[]{:S(2)}, u32[]{:S(2)}) async-start(bf16[8,16,2304]{2,1,0:T(8,128)(2,1)} %pad_maximum_fusion.2), calls=%async_computation.4 | async-start | bytes 1179648 | tf_op jit(solution)/shard_map/all_to_all | solution.py:202
  360.8 3.4 copy-start.37
  366.5 2.8 copy-start.53
  368.2 3.3 copy-start.10
  368.2 3.3 copy-start.23
  369.2 2.5 copy-start.32
  369.3 3.5 copy-start.51
  371.7 2.6 copy-start.13
  371.7 2.6 copy-start.21
  372.9 2.8 copy-start.49
  374.6 3.2 copy-start.12
  374.6 3.2 copy-start.19
  375.7 3.5 copy-start.47
  378.1 2.7 copy-start.17
  384.3 27.0 %collective-permute-start.6 = (bf16[128,768]{0,1:T(8,128)(2,1)S(1)}, bf16[128,768]{0,1:T(8,128)(2,1)S(1)}, u32[]{:S(2)}, u32[]{:S(2)}) collective-permute-start(bf16[128,768]{0,1:T(8,128)(2,1)S(1)} %get-tuple-element.2), channel_id=1, source_target_pairs={{0,2},{2,4},{4,6},{6,8},{8,10},{10,12},{12,14},{14,16},{16,18},{18... | collective-permute-start | bytes 589832 | tf_op jit(solution)/shard_map/ppermute | solution.py:20
  390.9 20.5 %collective-permute-start.7 = (bf16[128,768]{0,1:T(8,128)(2,1)S(1)}, bf16[128,768]{0,1:T(8,128)(2,1)S(1)}, u32[]{:S(2)}, u32[]{:S(2)}) collective-permute-start(bf16[128,768]{0,1:T(8,128)(2,1)S(1)} %get-tuple-element.3), channel_id=1, source_target_pairs={{2,0},{4,2},{6,4},{8,6},{10,8},{12,10},{14,12},{16,14},{18,16},{20... | collective-permute-start | bytes 589832 | tf_op jit(solution)/shard_map/ppermute | solution.py:22
  393.0 9.4 %copy-start.43 = (bf16[2,64,128]{2,1,0:T(8,128)(2,1)S(1)}, bf16[2,64,128]{2,1,0:T(8,128)(2,1)}, u32[]{:S(2)}) copy-start(bf16[2,64,128]{2,1,0:T(8,128)(2,1)} %fusion.47) | copy-start | bytes 98308
  393.0 9.4 %copy-start.42 = (bf16[2,64,128]{2,1,0:T(8,128)(2,1)S(1)}, bf16[2,64,128]{2,1,0:T(8,128)(2,1)}, u32[]{:S(2)}) copy-start(bf16[2,64,128]{2,1,0:T(8,128)(2,1)} %fusion.48) | copy-start | bytes 98308
  393.0 9.4 %copy-start.41 = (bf16[2,64,128]{2,1,0:T(8,128)(2,1)S(1)}, bf16[2,64,128]{2,1,0:T(8,128)(2,1)}, u32[]{:S(2)}) copy-start(bf16[2,64,128]{2,1,0:T(8,128)(2,1)} %fusion.49) | copy-start | bytes 98308
  393.0 9.4 %copy-start.40 = (bf16[2,64,128]{2,1,0:T(8,128)(2,1)S(1)}, bf16[2,64,128]{2,1,0:T(8,128)(2,1)}, u32[]{:S(2)}) copy-start(bf16[2,64,128]{2,1,0:T(8,128)(2,1)} %fusion.50) | copy-start | bytes 98308
  393.2 10.4 %collective-permute-start.4 = (bf16[128,768]{0,1:T(8,128)(2,1)S(1)}, bf16[128,768]{0,1:T(8,128)(2,1)S(1)}, u32[]{:S(2)}, u32[]{:S(2)}) collective-permute-start(bf16[128,768]{0,1:T(8,128)(2,1)S(1)} %get-tuple-element.4), channel_id=1, source_target_pairs={{0,2},{2,4},{4,6},{6,8},{8,10},{10,12},{12,14},{14,16},{16,18},{18... | collective-permute-start | bytes 589832 | tf_op jit(solution)/shard_map/ppermute | solution.py:20
  400.4 10.9 %collective-permute-start.5 = (bf16[128,768]{0,1:T(8,128)(2,1)S(1)}, bf16[128,768]{0,1:T(8,128)(2,1)S(1)}, u32[]{:S(2)}, u32[]{:S(2)}) collective-permute-start(bf16[128,768]{0,1:T(8,128)(2,1)S(1)} %get-tuple-element.5), channel_id=1, source_target_pairs={{2,0},{4,2},{6,4},{8,6},{10,8},{12,10},{14,12},{16,14},{18,16},{20... | collective-permute-start | bytes 589832 | tf_op jit(solution)/shard_map/ppermute | solution.py:22
  411.5 3.4 copy-start.56
  411.5 3.4 copy-start.58
  (25 other events, 32.1 us)
